TPU v7x, 256 devices: a whole 4x4x8 slice. The times are simulated.
256 devices in a mesh: ctx: 32 (over y, x, core), head: 8 (over z).
Axes of the slice: x: 4, y: 4, z: 8, core: 2. Of those that a mesh axis runs over, the one named last changes fastest.
Arguments:
- query_vectors: bfloat16 [4096, 4096], P('ctx', 'head'), may hold values from -6 to 6
- key_vectors: bfloat16 [4096, 4096], P('ctx', 'head'), may hold values from -1.5 to 1.5
- value_vectors: bfloat16 [4096, 4096], P('ctx', 'head'), may hold values from -6 to 6
- log_decay: float32 [32, 4096], P('head', 'ctx'), may hold values from -2 to 0, as said below
- residual: bfloat16 [4096, 3072], P('ctx'), may hold values from -6 to 6
- out_weight: bfloat16 [4096, 3072], P('head', 'ctx'), may hold values from -0.09375 to 0.09375
- attn_gain: float32 [4096], P('head'), may hold values from 0.1 to 1.9
- moe_gain: float32 [3072], replicated, may hold values from 0.1 to 1.9
- router: float32 [3072, 32], replicated, may hold values from -0.109375 to 0.109375
- w_gate: bfloat16 [32, 3072, 4608], P('ctx', None, 'head'), may hold values from -0.109375 to 0.109375
- w_up: bfloat16 [32, 3072, 4608], P('ctx', None, 'head'), may hold values from -0.109375 to 0.109375
- w_down: bfloat16 [32, 4608, 3072], P('ctx', 'head'), may hold values from -0.09375 to 0.09375
- expert_ids: int32 [4096, 2], P('ctx'), may hold values from 0 to 31, all different within a row; in each aligned block of 128 rows (0 to 127, 128 to 255, ...) at most 16 rows name the same one
Outputs:
- final_out: bfloat16 [4096, 3072], P('ctx', 'head')
Inputs may be any that keep to these rules, and one draw needn't show every extreme that they name: `expert_ids`: each row names 2 different experts. In each aligned block of 128 rows no expert is named by more than 16 rows, and in every draw some expert is named by exactly 16 rows of some block. `log_decay`: every entry is negative.
All inputs are finite; a program needn't handle non-finite values.
Results may differ from a plain program's by a relative error of at most 0.022.
Values may be sent and summed in bfloat16 or wider, within the bound.
No kernel may reach another device: no remote copies, remote signals or barrier semaphores. Data moves between devices by JAX's collectives and lax.ppermute only.
A program may use at most 128 MiB of HBM per device.

v0:
```python
import jax
import jax.numpy as jnp
from jax import lax
from jax.sharding import PartitionSpec as P

TOP = 2
PRECISE = lax.Precision.HIGHEST


def prior_states(final_log, local_state, axis):
    index = lax.axis_index(axis)
    totals = lax.all_gather(final_log, axis)
    states = lax.all_gather(local_state.astype(jnp.bfloat16), axis)
    peers = totals.shape[0]
    source = lax.broadcasted_iota(jnp.int32, (peers, peers), 0)
    between = lax.broadcasted_iota(jnp.int32, (peers, peers), 1)
    inside = (between > source) & (between < index)
    spans = jnp.sum(jnp.where(inside[:, :, None], totals[None, :, :], 0.0), axis=1)
    weights = jnp.where(jnp.arange(peers)[:, None] < index, jnp.exp(spans), 0.0)
    return jnp.einsum("jh,jhde->hde", weights, states.astype(jnp.float32), precision=PRECISE)


def local_attention(query_block, key_block, value_block, decay_block):
    running = jnp.cumsum(decay_block, axis=1)
    length_here = decay_block.shape[1]
    row_index = lax.broadcasted_iota(jnp.int32, (length_here, length_here), 0)
    col_index = lax.broadcasted_iota(jnp.int32, (length_here, length_here), 1)
    causal = (col_index <= row_index)[None]
    spread = jnp.where(causal, running[:, :, None] - running[:, None, :], 0.0)
    decay_weights = jnp.where(causal, jnp.exp(spread), 0.0)
    scores = jnp.einsum("htd,hsd->hts", query_block, key_block, precision=PRECISE) * decay_weights
    inside_part = jnp.einsum("hts,hse->hte", scores, value_block, precision=PRECISE)
    final_log = running[:, -1]
    tail_decay = jnp.exp(final_log[:, None] - running)
    local_state = jnp.einsum(
        "hsd,hse->hde", key_block * tail_decay[:, :, None], value_block, precision=PRECISE
    )
    return (inside_part, running, local_state, final_log)


def route_tokens(logits, expert_ids, experts_total):
    onehot = expert_ids[:, :, None] == lax.broadcasted_iota(jnp.int32, (1, 1, experts_total), 2)
    chosen = jnp.sum(jnp.where(onehot, logits[:, None, :], 0.0), axis=2)
    leading = jax.nn.sigmoid(chosen[:, 0] - chosen[:, 1])
    gate_weights = jnp.stack([leading, 1.0 - leading], axis=1)
    marked = onehot.reshape(-1, experts_total).astype(jnp.int32)
    earlier = jnp.cumsum(marked, axis=0) - marked
    slot_index = jnp.sum(earlier * marked, axis=1).reshape(expert_ids.shape)
    return (gate_weights, slot_index)


def body(
    query_vectors,
    key_vectors,
    value_vectors,
    log_decay,
    residual,
    out_weight,
    attn_gain,
    moe_gain,
    router,
    w_gate,
    w_up,
    w_down,
    expert_ids,
):
    token_count = query_vectors.shape[0]
    heads_here = log_decay.shape[0]
    head_size = query_vectors.shape[1] // heads_here

    def split_heads(matrix_in):
        return (
            matrix_in.astype(jnp.float32)
            .reshape(token_count, heads_here, head_size)
            .transpose(1, 0, 2)
        )

    query_heads = split_heads(query_vectors)
    inside_part, running, local_state, final_log = local_attention(
        query_heads, split_heads(key_vectors), split_heads(value_vectors), log_decay
    )
    prior_state = prior_states(final_log, local_state, "ctx")
    outside_part = jnp.exp(running)[:, :, None] * jnp.einsum(
        "htd,hde->hte", query_heads, prior_state, precision=PRECISE
    )
    attended = inside_part + outside_part
    square_mean = jnp.mean(attended * attended, axis=2, keepdims=True)
    heads_normed = (
        attended * lax.rsqrt(square_mean + 1e-05) * attn_gain.reshape(heads_here, 1, head_size)
    )
    heads_normed = (
        heads_normed.astype(jnp.bfloat16)
        .transpose(1, 0, 2)
        .reshape(token_count, heads_here * head_size)
    )
    partial_out = jnp.dot(
        heads_normed,
        lax.all_gather(out_weight, "ctx", axis=1, tiled=True),
        preferred_element_type=jnp.float32,
    )
    model_width = residual.shape[1]
    experts_total = router.shape[1]
    capacity = 2 * token_count * TOP // experts_total
    slice_width = model_width // lax.axis_size("head")
    slice_start = lax.axis_index("head") * slice_width
    projected = lax.psum(partial_out.astype(jnp.bfloat16), "head").astype(jnp.float32)
    mixed_rows = (residual.astype(jnp.float32) + projected).astype(jnp.bfloat16)
    mixed_wide = mixed_rows.astype(jnp.float32)
    inv_rms = lax.rsqrt(jnp.mean(mixed_wide * mixed_wide, axis=1, keepdims=True) + 1e-06)
    scaled = mixed_wide * moe_gain[None, :]
    moe_in = (scaled * inv_rms).astype(jnp.bfloat16)
    logits = inv_rms * jnp.dot(scaled, router, precision=PRECISE)
    base_slice = lax.dynamic_slice_in_dim(mixed_wide, slice_start, slice_width, 1)
    gate_weights, slot_index = route_tokens(logits, expert_ids, experts_total)
    target = (expert_ids * capacity + slot_index).reshape(-1)
    width_here = moe_in.shape[1]
    source = jnp.repeat(moe_in, TOP, axis=0)
    packed = jnp.zeros((experts_total * capacity, width_here), jnp.bfloat16).at[target].set(source)
    arrived = lax.all_to_all(
        packed.reshape(experts_total, capacity, width_here),
        "ctx",
        split_axis=0,
        concat_axis=0,
        tiled=True,
    )
    flat_rows = arrived.reshape(-1, model_width)
    gate_part = jnp.dot(flat_rows, w_gate[0], preferred_element_type=jnp.float32)
    up_part = jnp.dot(flat_rows, w_up[0], preferred_element_type=jnp.float32)
    hidden = (jax.nn.silu(gate_part) * up_part).astype(jnp.bfloat16)
    partial_down = jnp.dot(hidden, w_down[0], preferred_element_type=jnp.float32)
    summed = lax.psum_scatter(
        partial_down.astype(jnp.bfloat16), "head", scatter_dimension=1, tiled=True
    )
    returned = lax.all_to_all(
        summed.reshape(experts_total, capacity, slice_width),
        "ctx",
        split_axis=0,
        concat_axis=0,
        tiled=True,
    )
    lookup = returned.reshape(experts_total * capacity, slice_width)
    picked = lookup[target].reshape(token_count, TOP, slice_width).astype(jnp.float32)
    final_out = (
        base_slice + gate_weights[:, 0:1] * picked[:, 0] + gate_weights[:, 1:2] * picked[:, 1]
    )
    return final_out.astype(jnp.bfloat16)


def solution(mesh):
    in_specs = (
        P("ctx", "head"),
        P("ctx", "head"),
        P("ctx", "head"),
        P("head", "ctx"),
        P("ctx", None),
        P("head", "ctx"),
        P("head"),
        P(),
        P(),
        P("ctx", None, "head"),
        P("ctx", None, "head"),
        P("ctx", "head", None),
        P("ctx", None),
    )
    out_specs = P("ctx", "head")
    return jax.shard_map(body, mesh=mesh, in_specs=in_specs, out_specs=out_specs, check_vma=False)
```

profile of v0, /device:TPU:1, one launch (start us, length us, event | category | flops | bytes accessed | tf_op | source)
XLA Modules:
  0.0 356.7 jit_solution(9251623039175811909)
XLA Ops:
  6.5 1.1 reduce_window_sum.26
  8.5 1.7 copy.78
  10.1 1.9 convolution_convert_fusion.2
  12.1 0.7 all-gather.5.cloned.1.call-update
  12.8 1.3 dynamic-slice
  15.0 66.0 %all-reduce = f32[128]{0:T(128)} all-reduce(f32[128]{0:T(128)S(1)} %dynamic-update-slice), channel_id=2, replica_groups=mesh['ctx'=32,'head'=8] {'ctx'}, use_global_device_ids=true, to_apply=%add | all-reduce | flops 128 | bytes 1024
  81.0 0.7 reshape.188
  81.8 0.7 copy.65
  82.4 1.4 copy.66
  83.8 1.6 eq.39
  85.4 0.8 select_reduce_fusion
  86.2 1.9 convolution_multiply_fusion
  88.1 5.7 %fusion = f32[4,1,128,128]{3,1,2,0:T(1,128)S(1)} fusion(f32[32,4,1,1]{0,2,3,1:T(1,128)S(1)} %bitcast.151, bf16[32,4,128,128]{3,2,1,0:T(8,128)(2,1)} %bitcast.142), kind=kOutput, calls=%fused_computation.3 | convolution fusion | flops 25165824 | bytes 4456960 | tf_op jit(solution)/shard_map/jh,jhde->hde/dot_general | solution.py:20
  94.8 0.8 fusion.30
  95.6 23.6 %all-gather.5.cloned.1.call-done = bf16[512,3072]{0,1:T(8,128)(2,1)} async-done(((bf16[512,96]{0,1:T(8,128)(2,1)}), bf16[512,3072]{0,1:T(8,128)(2,1)}) %all-gather.5.cloned.1.call-update) | async-done | bytes 3145744 | tf_op jit(solution)/shard_map/all_gather | solution.py:98
  119.2 4.0 %convolution_convert_fusion.1 = bf16[128,3072]{1,0:T(8,128)(2,1)} fusion(bf16[128,512]{0,1:T(8,128)(2,1)} %bitcast.147, bf16[512,3072]{0,1:T(8,128)(2,1)} %all-gather.5.cloned.1.call-done), kind=kOutput, calls=%fused_computation.5 | convolution fusion | flops 403046400 | bytes 4063232 | tf_op jit(solution)/shard_map/dot_general | solution.py:96
  123.5 1.3 fusion.48
  124.8 1.5 eq.35
  126.3 1.9 reduce-window.6
  128.2 1.5 slice_reduce_fusion
  129.7 1.3 reduce-window.9
  131.6 1.4 fusion.47
  133.1 1.4 reshape.164
  134.5 1.5 copy.69
  136.0 1.2 multiply_add_fusion
  137.2 1.4 copy.70
  138.6 1.5 reshape.165
  140.1 1.2 compare_select_fusion
  141.3 51.4 %all-reduce.3.cloned.1.call-done = bf16[128,3072]{1,0:T(8,128)(2,1)} async-done(((bf16[128,3072]{1,0:T(8,128)(2,1)}), bf16[128,3072]{1,0:T(8,128)(2,1)}) %all-reduce.3.cloned.1.call-update) | async-done | bytes 786448 | tf_op jit(solution)/shard_map/psum | solution.py:106
  192.7 2.7 fusion.51
  197.1 2.0 broadcast_in_dim.93
  199.1 4.6 %reshape.184 = bf16[256,3072]{1,0:T(8,128)(2,1)} reshape(bf16[128,2,3072]{2,1,0:T(2,128)(2,1)} %broadcast_in_dim.93) | data formatting | bytes 3145728 | tf_op jit(solution)/shard_map/reshape | solution.py:117
  203.7 5.8 %scatter_custom_fusion = bf16[512,3072]{1,0:T(8,128)(2,1)} fusion(s32[256]{0:T(256)} %bitcast.152, bf16[256,3072]{1,0:T(8,128)(2,1)} %reshape.184, bf16[]{:T(256)} %constant.42.clone.1), kind=kCustom, calls=%fused_computation.12 | custom fusion | bytes 3146240 | tf_op jit(solution)/shard_map/scatter | solution.py:118
  209.4 51.8 %all_to_all.10 = bf16[32,16,3072]{2,1,0:T(8,128)(2,1)S(1)} all-to-all(bf16[32,16,3072]{2,1,0:T(8,128)(2,1)} %bitcast.141), channel_id=1, replica_groups=mesh['ctx'=32,'head'=8] {'ctx'}, dimensions={0} | all-to-all | bytes 6291456 | tf_op jit(solution)/shard_map/all_to_all | solution.py:119
  261.2 1.7 copy-done.2
  262.9 3.1 fusion.5
  266.1 9.5 %convolution_convert_fusion = bf16[512,3072]{1,0:T(8,128)(2,1)} fusion(bf16[1,576,3072]{2,1,0:T(8,128)(2,1)S(1)} %copy-done, bf16[512,3072]{1,0:T(8,128)(2,1)} %bitcast.144, bf16[1,3072,576]{1,2,0:T(8,128)(2,1)} %param.23, f32[512,576]{0,1:T(8,128)} %fusion.5), kind=kOutput, calls=%fused_computation.2 | convolution fusion | flops 3627220992 | bytes 14548992 | tf_op jit(solution)/shard_map/dot_general | solution.py:130
  275.6 4.7 %copy.81 = bf16[512,3072]{0,1:T(8,128)(2,1)} copy(bf16[512,3072]{1,0:T(8,128)(2,1)} %convolution_convert_fusion) | data formatting | bytes 6291456
  280.3 1.2 pad_clamp_fusion
  281.5 37.5 %reduce-scatter.4.cloned.1.call-done = bf16[384,512]{1,0:T(8,128)(2,1)} async-done(((bf16[3072,512]{1,0:T(8,128)(2,1)}), bf16[384,512]{1,0:T(8,128)(2,1)}) %reduce-scatter.4.cloned.1.call-update) | async-done | bytes 393232
  319.0 2.0 copy.82
  321.0 11.0 %all-to-all-start.1 = ((bf16[32,16,384]{2,1,0:T(8,128)(2,1)}), bf16[32,16,384]{2,1,0:T(8,128)(2,1)}, u32[]{:S(2)}, u32[]{:S(2)}) async-start(bf16[32,16,384]{2,1,0:T(8,128)(2,1)} %bitcast.145), calls=%async_computation.1 | async-start | bytes 786432 | tf_op jit(solution)/shard_map/all_to_all | solution.py:134
  332.0 2.8 fusion.18
  334.8 7.4 %all-to-all-done.1 = bf16[32,16,384]{2,1,0:T(8,128)(2,1)} async-done(((bf16[32,16,384]{2,1,0:T(8,128)(2,1)}), bf16[32,16,384]{2,1,0:T(8,128)(2,1)}, u32[]{:S(2)}, u32[]{:S(2)}) %all-to-all-start.1) | async-done | bytes 393248 | tf_op jit(solution)/shard_map/all_to_all | solution.py:134
  342.2 3.0 gather_fusion
  345.2 1.9 reshape.171
  347.0 1.5 fusion.52
  348.5 1.7 fusion.35
  (52 shorter events, 4.7 us)
Async XLA Ops:
  6.5 259.6 %copy-start = (bf16[1,576,3072]{2,1,0:T(8,128)(2,1)S(1)}, bf16[1,576,3072]{2,1,0:T(8,128)(2,1)}, u32[]{:S(2)}) copy-start(bf16[1,576,3072]{2,1,0:T(8,128)(2,1)} %param.24) | copy-start | bytes 10616836
  6.5 81.6 %all-gather.7.cloned.1.call-start = ((), (), s32[]{:S(2)}) async-start(), calls=%async_computation.5 | async-start | bytes 4325376 | tf_op jit(solution)/shard_map/all_gather | solution.py:13
  7.7 7.3 %copy-start.7 = (f32[4,128]{1,0:T(4,128)}, f32[4,128]{1,0:T(4,128)S(1)}, u32[]{:S(2)}) copy-start(f32[4,128]{1,0:T(4,128)S(1)} %reduce_window_sum.26) | copy-start | bytes 6148
  12.0 107.2 %all-gather.5.cloned.1.call-start = ((), (), s32[]{:S(2)}) async-start(), calls=%async_computation.3 | async-start | bytes 3244032 | tf_op jit(solution)/shard_map/all_gather | solution.py:98
  12.8 179.9 %all-reduce.3.cloned.1.call-start = ((), (), s32[]{:S(2)}) async-start(), calls=%async_computation.4 | async-start | bytes 1572864 | tf_op jit(solution)/shard_map/psum | solution.py:106
  82.4 11.8 %copy-start.10 = (f32[4,128]{1,0:T(4,128)S(1)}, f32[4,128]{1,0:T(4,128)}, u32[]{:S(2)}) copy-start(f32[4,128]{1,0:T(4,128)} %get-tuple-element.12) | copy-start | bytes 6148
  88.1 6.7 %copy-start.9 = (f32[128,4]{0,1:T(4,128)S(1)}, f32[128,4]{0,1:T(4,128)}, u32[]{:S(2)}) copy-start(f32[128,4]{0,1:T(4,128)} %get-tuple-element.11) | copy-start | bytes 6148
  88.1 5.8 %copy-start.5 = (bf16[128,512]{1,0:T(8,128)(2,1)S(1)}, bf16[128,512]{1,0:T(8,128)(2,1)}, u32[]{:S(2)}) copy-start(bf16[128,512]{1,0:T(8,128)(2,1)} %param.13) | copy-start | bytes 393220
  88.1 6.2 %copy-start.3 = (bf16[128,512]{1,0:T(8,128)(2,1)S(1)}, bf16[128,512]{1,0:T(8,128)(2,1)}, u32[]{:S(2)}) copy-start(bf16[128,512]{1,0:T(8,128)(2,1)} %param.15) | copy-start | bytes 393220
  88.1 6.2 %copy-start.4 = (f32[4,128,128]{2,1,0:T(8,128)S(1)}, f32[4,128,128]{2,1,0:T(8,128)}, u32[]{:S(2)}) copy-start(f32[4,128,128]{2,1,0:T(8,128)} %convolution_multiply_fusion) | copy-start | bytes 786436
  88.1 6.7 %copy-start.11 = (f32[512]{0:T(512)S(1)}, f32[512]{0:T(512)}, u32[]{:S(2)}) copy-start(f32[512]{0:T(512)} %param.19) | copy-start | bytes 6148
  94.8 41.2 %copy-start.8 = (s32[128,2]{0,1:T(2,128)S(1)}, s32[128,2]{0,1:T(2,128)}, u32[]{:S(2)}) copy-start(s32[128,2]{0,1:T(2,128)} %param.25) | copy-start | bytes 3076
  123.2 73.6 %copy-start.6 = (f32[3072]{0:T(1024)S(1)}, f32[3072]{0:T(1024)}, u32[]{:S(2)}) copy-start(f32[3072]{0:T(1024)} %param.20) | copy-start | bytes 36868
  123.3 195.8 %reduce-scatter.4.cloned.1.call-start = ((), (), s32[]{:S(2)}) async-start(), calls=%async_computation.6 | async-start | bytes 3538944
  195.4 0.9 copy-start.1
  196.3 0.5 copy-start.12
  209.4 53.5 %copy-start.13 = (bf16[1,3072,576]{1,2,0:T(8,128)(2,1)S(1)}, bf16[1,3072,576]{1,2,0:T(8,128)(2,1)}, u32[]{:S(2)}) copy-start(bf16[1,3072,576]{1,2,0:T(8,128)(2,1)} %param.22) | copy-start | bytes 10616836
  261.2 1.7 copy-start.2
  321.0 21.2 %all-to-all-start.1 = ((bf16[32,16,384]{2,1,0:T(8,128)(2,1)}), bf16[32,16,384]{2,1,0:T(8,128)(2,1)}, u32[]{:S(2)}, u32[]{:S(2)}) async-start(bf16[32,16,384]{2,1,0:T(8,128)(2,1)} %bitcast.145), calls=%async_computation.1 | async-start | bytes 786432 | tf_op jit(solution)/shard_map/all_to_all | solution.py:134
Sparse Core Ops, SparseCore 0:
  12.1 55.2 all-gather.6
  70.0 49.2 all-gather.4
  123.4 69.2 all-reduce.2
  280.4 38.5 reduce-scatter.3
where the time goes:
time: 358 us; the launch traced here: 357 us
  waiting for transfers between devices  121 us (34%)
  blocking collectives  118 us (33%)
  local copies, waits for them, and re-layouts  45.6 us (13%)
  matrix products  29.8 us (8%)
  other arithmetic  17.7 us (5%)
  between operations  14 us (4%)
  starting transfers between devices  11.3 us (3%)
    unnamed x1, blocking collectives  66 us
    all_to_all x1, blocking collectives, body(): lax.all_to_all(packed.reshape(experts_total, capacity, width_here), 'ctx'...  51.8 us
    psum x1, waiting for transfers between devices, body(): lax.psum(partial_out.astype(jnp.bfloat16), 'head').astype(jnp.float32)  51.4 us
    unnamed x5, waiting for transfers between devices  38.2 us
    all_gather x1, waiting for transfers between devices, body(): lax.all_gather(out_weight, 'ctx', axis=1, tiled=True)  23.6 us
    unnamed x34, local copies, waits for them, and re-layouts  12.5 us
    all_to_all x1, starting transfers between devices, body(): lax.all_to_all(summed.reshape(experts_total, capacity, slice_width), 'ctx...  11 us
    dot_general x1, matrix products, body(): jnp.dot(hidden, w_down[0], preferred_element_type=jnp.float32)  9.52 us
  transfers between devices with their start and end apart: 5, of which 4 were waited for; matrix products, arithmetic and copies ran while one was open for 11% of the time, Pallas kernels for 0%

commit v1 on v0

--- a/solution.py
+++ b/solution.py
@@ -95,7 +95,9 @@
     )
     partial_out = jnp.dot(
         heads_normed,
-        lax.all_gather(out_weight, "ctx", axis=1, tiled=True),
+        jnp.concatenate(
+            lax.all_to_all(jnp.stack([out_weight] * lax.axis_size("ctx")), "ctx", 0, 0), axis=1
+        ),
         preferred_element_type=jnp.float32,
     )
     model_width = residual.shape[1]

time: 358 us -> 373 us (1.042)
  blocking collectives: 118 us -> 145 us
  waiting for transfers between devices: 121 us -> 97.1 us
  starting transfers between devices: 11.3 us -> 19.6 us
    unnamed x1, blocking collectives: 66 us -> 93.4 us
    all_gather x1 -> x0, waiting for transfers between devices: 23.6 us -> none  [body(): lax.all_gather(out_weight, 'ctx', axis=1, tiled=True)]
    all_to_all x0 -> x1, starting transfers between devices: none -> 8.76 us  [body(): lax.all_to_all(jnp.stack([out_weight] * lax.axis_size('ctx')), 'ctx', 0, 0)]
    unnamed x34 -> x36, local copies, waits for them, and re-layouts: 12.5 us -> 11.9 us
    unnamed x5 -> x4, waiting for transfers between devices: 38.2 us -> 37.7 us
  transfers between devices with their start and end apart: 5 -> 5, of which waited for: 4 -> 3; matrix products, arithmetic and copies ran while one was open for 11% -> 11% of each run, Pallas kernels for 0% -> 0%
where the time goes in v1:
time: 373 us; the launch traced here: 371 us
  blocking collectives  145 us (39%)
  waiting for transfers between devices  97.1 us (26%)
  local copies, waits for them, and re-layouts  47.8 us (13%)
  matrix products  29.8 us (8%)
  starting transfers between devices  19.6 us (5%)
  other arithmetic  17.7 us (5%)
  between operations  14 us (4%)
    unnamed x1, blocking collectives  93.4 us
    psum x1, waiting for transfers between devices, body(): lax.psum(partial_out.astype(jnp.bfloat16), 'head').astype(jnp.float32)  52 us
    all_to_all x1, blocking collectives, body(): lax.all_to_all(packed.reshape(experts_total, capacity, width_here), 'ctx'...  51.8 us
    unnamed x4, waiting for transfers between devices  37.7 us
    unnamed x36, local copies, waits for them, and re-layouts  11.9 us
    all_to_all x1, starting transfers between devices, body(): lax.all_to_all(summed.reshape(experts_total, capacity, slice_width), 'ctx...  10.6 us
    dot_general x1, matrix products, body(): jnp.dot(hidden, w_down[0], preferred_element_type=jnp.float32)  9.52 us
    all_to_all x1, starting transfers between devices, body(): lax.all_to_all(jnp.stack([out_weight] * lax.axis_size('ctx')), 'ctx', 0, 0)  8.76 us
  transfers between devices with their start and end apart: 5, of which 3 were waited for; matrix products, arithmetic and copies ran while one was open for 11% of the time, Pallas kernels for 0%

profile of v1, /device:TPU:1, one launch (start us, length us, event | category | flops | bytes accessed | tf_op | source)
XLA Modules:
  0.0 371.2 jit_solution(14964918147618845600)
XLA Ops:
  6.5 1.1 reduce_window_sum.26
  8.5 1.7 copy.79
  10.1 1.9 convolution_convert_fusion.2
  12.0 3.0 stack.2
  15.0 8.8 %all-to-all-start = ((bf16[32,512,96]{1,2,0:T(8,128)(2,1)}), bf16[32,512,96]{1,2,0:T(8,128)(2,1)}, u32[]{:S(2)}, u32[]{:S(2)}) async-start(bf16[32,512,96]{1,2,0:T(8,128)(2,1)} %stack.2), calls=%async_computation | async-start | bytes 6291456 | tf_op jit(solution)/shard_map/all_to_all | solution.py:99
  25.3 93.4 %all-reduce = f32[128]{0:T(128)} all-reduce(f32[128]{0:T(128)S(1)} %dynamic-update-slice), channel_id=2, replica_groups=mesh['ctx'=32,'head'=8] {'ctx'}, use_global_device_ids=true, to_apply=%add | all-reduce | flops 128 | bytes 1024
  118.7 0.7 reshape.198
  120.1 1.4 copy.67
  121.5 1.6 eq.39
  123.1 0.8 select_reduce_fusion
  123.9 1.9 convolution_multiply_fusion
  125.8 5.7 %fusion = f32[4,1,128,128]{3,1,2,0:T(1,128)S(1)} fusion(f32[32,4,1,1]{0,2,3,1:T(1,128)S(1)} %bitcast.154, bf16[32,4,128,128]{3,2,1,0:T(8,128)(2,1)} %bitcast.145), kind=kOutput, calls=%fused_computation.3 | convolution fusion | flops 25165824 | bytes 4456960 | tf_op jit(solution)/shard_map/jh,jhde->hde/dot_general | solution.py:20
  132.5 0.8 fusion.30
  133.3 4.0 %convolution_convert_fusion.1 = bf16[128,3072]{1,0:T(8,128)(2,1)} fusion(bf16[128,512]{0,1:T(8,128)(2,1)} %bitcast.150, bf16[512,3072]{0,1:T(8,128)(2,1)} %bitcast.20), kind=kOutput, calls=%fused_computation.5 | convolution fusion | flops 403046400 | bytes 4063232 | tf_op jit(solution)/shard_map/dot_general | solution.py:96
  137.5 1.3 fusion.48
  138.8 1.5 eq.35
  140.4 1.9 reduce-window.6
  142.3 1.5 slice_reduce_fusion
  143.8 1.3 reduce-window.9
  145.0 0.7 slice.28
  145.7 1.4 fusion.47
  147.1 1.4 reshape.174
  148.6 1.5 copy.70
  150.1 1.2 multiply_add_fusion
  151.3 1.4 copy.71
  152.7 1.5 reshape.175
  154.2 1.2 compare_select_fusion
  155.4 52.0 %all-reduce.3.cloned.1.call-done = bf16[128,3072]{1,0:T(8,128)(2,1)} async-done(((bf16[128,3072]{1,0:T(8,128)(2,1)}), bf16[128,3072]{1,0:T(8,128)(2,1)}) %all-reduce.3.cloned.1.call-update) | async-done | bytes 786448 | tf_op jit(solution)/shard_map/psum | solution.py:108
  207.4 2.7 fusion.51
  210.4 0.7 copy-done.1
  211.8 2.0 broadcast_in_dim.93
  213.8 4.6 %reshape.194 = bf16[256,3072]{1,0:T(8,128)(2,1)} reshape(bf16[128,2,3072]{2,1,0:T(2,128)(2,1)} %broadcast_in_dim.93) | data formatting | bytes 3145728 | tf_op jit(solution)/shard_map/reshape | solution.py:119
  218.4 5.8 %scatter_custom_fusion = bf16[512,3072]{1,0:T(8,128)(2,1)} fusion(s32[256]{0:T(256)} %bitcast.155, bf16[256,3072]{1,0:T(8,128)(2,1)} %reshape.194, bf16[]{:T(256)} %constant.42.clone.1), kind=kCustom, calls=%fused_computation.12 | custom fusion | bytes 3146240 | tf_op jit(solution)/shard_map/scatter | solution.py:120
  224.2 51.8 %all_to_all.15 = bf16[32,16,3072]{2,1,0:T(8,128)(2,1)S(1)} all-to-all(bf16[32,16,3072]{2,1,0:T(8,128)(2,1)} %bitcast.144), channel_id=1, replica_groups=mesh['ctx'=32,'head'=8] {'ctx'}, dimensions={0} | all-to-all | bytes 6291456 | tf_op jit(solution)/shard_map/all_to_all | solution.py:121
  276.0 1.7 copy-done.2
  277.7 3.2 fusion.5
  280.8 9.5 %convolution_convert_fusion = bf16[512,3072]{1,0:T(8,128)(2,1)} fusion(bf16[1,576,3072]{2,1,0:T(8,128)(2,1)S(1)} %copy-done, bf16[512,3072]{1,0:T(8,128)(2,1)} %bitcast.147, bf16[1,3072,576]{1,2,0:T(8,128)(2,1)} %param.23, f32[512,576]{0,1:T(8,128)} %fusion.5), kind=kOutput, calls=%fused_computation.2 | convolution fusion | flops 3627220992 | bytes 14548992 | tf_op jit(solution)/shard_map/dot_general | solution.py:132
  290.3 4.7 %copy.82 = bf16[512,3072]{0,1:T(8,128)(2,1)} copy(bf16[512,3072]{1,0:T(8,128)(2,1)} %convolution_convert_fusion) | data formatting | bytes 6291456
  295.1 1.2 pad_clamp_fusion
  296.3 37.6 %reduce-scatter.4.cloned.1.call-done = bf16[384,512]{1,0:T(8,128)(2,1)} async-done(((bf16[3072,512]{1,0:T(8,128)(2,1)}), bf16[384,512]{1,0:T(8,128)(2,1)}) %reduce-scatter.4.cloned.1.call-update) | async-done | bytes 393232
  333.9 2.0 copy.83
  335.9 10.6 %all-to-all-start.2 = ((bf16[32,16,384]{2,1,0:T(8,128)(2,1)}), bf16[32,16,384]{2,1,0:T(8,128)(2,1)}, u32[]{:S(2)}, u32[]{:S(2)}) async-start(bf16[32,16,384]{2,1,0:T(8,128)(2,1)} %bitcast.148), calls=%async_computation.2 | async-start | bytes 786432 | tf_op jit(solution)/shard_map/all_to_all | solution.py:136
  346.4 2.8 fusion.18
  349.3 7.4 %all-to-all-done.2 = bf16[32,16,384]{2,1,0:T(8,128)(2,1)} async-done(((bf16[32,16,384]{2,1,0:T(8,128)(2,1)}), bf16[32,16,384]{2,1,0:T(8,128)(2,1)}, u32[]{:S(2)}, u32[]{:S(2)}) %all-to-all-start.2) | async-done | bytes 393248 | tf_op jit(solution)/shard_map/all_to_all | solution.py:136
  356.6 3.0 gather_fusion
  359.6 1.9 reshape.181
  361.5 1.5 fusion.52
  362.9 1.7 fusion.35
  (54 shorter events, 4.5 us)
Async XLA Ops:
  6.5 274.3 %copy-start = (bf16[1,576,3072]{2,1,0:T(8,128)(2,1)S(1)}, bf16[1,576,3072]{2,1,0:T(8,128)(2,1)}, u32[]{:S(2)}) copy-start(bf16[1,576,3072]{2,1,0:T(8,128)(2,1)} %param.24) | copy-start | bytes 10616836
  6.5 119.3 %all-gather.4.cloned.1.call-start = ((), (), s32[]{:S(2)}) async-start(), calls=%async_computation.5 | async-start | bytes 4325376 | tf_op jit(solution)/shard_map/all_gather | solution.py:13
  7.7 7.3 %copy-start.7 = (f32[4,128]{1,0:T(4,128)}, f32[4,128]{1,0:T(4,128)S(1)}, u32[]{:S(2)}) copy-start(f32[4,128]{1,0:T(4,128)S(1)} %reduce_window_sum.26) | copy-start | bytes 6148
  15.0 8.8 %copy-start.14 = (u32[256]{0:T(256)S(1)}, u32[256]{0:T(256)}, u32[]{:S(2)}) copy-start(u32[256]{0:T(256)} %constant.51) | copy-start | bytes 3076
  15.0 118.3 %all-to-all-start = ((bf16[32,512,96]{1,2,0:T(8,128)(2,1)}), bf16[32,512,96]{1,2,0:T(8,128)(2,1)}, u32[]{:S(2)}, u32[]{:S(2)}) async-start(bf16[32,512,96]{1,2,0:T(8,128)(2,1)} %stack.2), calls=%async_computation | async-start | bytes 6291456 | tf_op jit(solution)/shard_map/all_to_all | solution.py:99
  23.8 183.6 %all-reduce.3.cloned.1.call-start = ((), (), s32[]{:S(2)}) async-start(), calls=%async_computation.4 | async-start | bytes 1572864 | tf_op jit(solution)/shard_map/psum | solution.py:108
  120.1 11.9 %copy-start.10 = (f32[4,128]{1,0:T(4,128)S(1)}, f32[4,128]{1,0:T(4,128)}, u32[]{:S(2)}) copy-start(f32[4,128]{1,0:T(4,128)} %get-tuple-element.12) | copy-start | bytes 6148
  125.8 6.7 %copy-start.9 = (f32[128,4]{0,1:T(4,128)S(1)}, f32[128,4]{0,1:T(4,128)}, u32[]{:S(2)}) copy-start(f32[128,4]{0,1:T(4,128)} %get-tuple-element.11) | copy-start | bytes 6148
  125.8 5.8 %copy-start.5 = (bf16[128,512]{1,0:T(8,128)(2,1)S(1)}, bf16[128,512]{1,0:T(8,128)(2,1)}, u32[]{:S(2)}) copy-start(bf16[128,512]{1,0:T(8,128)(2,1)} %param.13) | copy-start | bytes 393220
  125.8 6.2 %copy-start.3 = (bf16[128,512]{1,0:T(8,128)(2,1)S(1)}, bf16[128,512]{1,0:T(8,128)(2,1)}, u32[]{:S(2)}) copy-start(bf16[128,512]{1,0:T(8,128)(2,1)} %param.15) | copy-start | bytes 393220
  125.8 6.2 %copy-start.4 = (f32[4,128,128]{2,1,0:T(8,128)S(1)}, f32[4,128,128]{2,1,0:T(8,128)}, u32[]{:S(2)}) copy-start(f32[4,128,128]{2,1,0:T(8,128)} %convolution_multiply_fusion) | copy-start | bytes 786436
  125.8 6.7 %copy-start.11 = (f32[512]{0:T(512)S(1)}, f32[512]{0:T(512)}, u32[]{:S(2)}) copy-start(f32[512]{0:T(512)} %param.19) | copy-start | bytes 6148
  132.4 17.6 %copy-start.8 = (s32[128,2]{0,1:T(2,128)S(1)}, s32[128,2]{0,1:T(2,128)}, u32[]{:S(2)}) copy-start(s32[128,2]{0,1:T(2,128)} %param.25) | copy-start | bytes 3076
  137.3 74.3 %copy-start.6 = (f32[3072]{0:T(1024)S(1)}, f32[3072]{0:T(1024)}, u32[]{:S(2)}) copy-start(f32[3072]{0:T(1024)} %param.20) | copy-start | bytes 36868
  137.3 196.6 %reduce-scatter.4.cloned.1.call-start = ((), (), s32[]{:S(2)}) async-start(), calls=%async_computation.6 | async-start | bytes 3538944
  210.1 0.9 copy-start.1
  211.1 0.5 copy-start.12
  224.2 53.5 %copy-start.13 = (bf16[1,3072,576]{1,2,0:T(8,128)(2,1)S(1)}, bf16[1,3072,576]{1,2,0:T(8,128)(2,1)}, u32[]{:S(2)}) copy-start(bf16[1,3072,576]{1,2,0:T(8,128)(2,1)} %param.22) | copy-start | bytes 10616836
  276.0 1.7 copy-start.2
  335.9 20.8 %all-to-all-start.2 = ((bf16[32,16,384]{2,1,0:T(8,128)(2,1)}), bf16[32,16,384]{2,1,0:T(8,128)(2,1)}, u32[]{:S(2)}, u32[]{:S(2)}) async-start(bf16[32,16,384]{2,1,0:T(8,128)(2,1)} %bitcast.148), calls=%async_computation.2 | async-start | bytes 786432 | tf_op jit(solution)/shard_map/all_to_all | solution.py:136
Sparse Core Ops, SparseCore 0:
  12.2 78.7 all-gather.3
  137.4 69.9 all-reduce.2
  295.2 38.6 reduce-scatter.3
